TPU v7x, 32 devices: a whole 2x2x4 slice. The times are simulated.
32 devices in a mesh: dom: 8 (over y, x, core), sub: 4 (over z).
Axes of the slice: x: 2, y: 2, z: 4, core: 2. Of those that a mesh axis runs over, the one named last changes fastest.
Arguments:
- vectors: bfloat16 [8192, 1024], P(('dom', 'sub')), may hold values from -8 to 8
- assign: int32 [8192], P(('dom', 'sub')), may hold values from 0 to 32767, as said below
- codes: int32 [8192, 256], P(('dom', 'sub')), may hold values from 0 to 15
- centroids: float32 [32768, 1024], P('dom', 'sub'), may hold values from -4 to 4
- perp_ratio: float32 [32768], P('dom'), may hold values from 0.25 to 0.9
- codebook: float32 [256, 16, 4], P('sub'), may hold values from -4 to 4
- codeword_weight_total: float32 [256, 16], P('sub'), may hold values from 64 to 512
Outputs:
- new_centroids: float32 [32768, 1024], P('dom', 'sub')
- residual: bfloat16 [8192, 1024], P(('dom', 'sub'))
- new_codebook: float32 [256, 16, 4], P('sub')
Inputs may be any that keep to these rules, and one draw needn't show every extreme that they name: `assign`: owner o holds partitions o * 4096 to (o + 1) * 4096 - 1 and o runs over 8 owners. The rows of one device are grouped by owner in increasing owner order; at most 64 rows of one device belong to one owner, and on every device some owner receives exactly 64.
All inputs are finite; a program needn't handle non-finite values.
Results may differ from a plain program's by a relative error of at most 0.001.
Values may be sent and summed in bfloat16 or wider, within the bound.
No kernel may reach another device: no remote copies, remote signals or barrier semaphores. Data moves between devices by JAX's collectives and lax.ppermute only.
A program may use at most 128 MiB of HBM per device.

v0:
```python
import jax
import jax.numpy as jnp
from jax import lax
from jax.sharding import PartitionSpec as P

K = 16
DS = 4
ITERS = 4


def per_device(vectors, assign, codes, centroids, perp_ratio, codebook, codeword_weight_total):
    owners = lax.axis_size("dom")
    sub_count = lax.axis_size("sub")
    rows_dev, row_width = vectors.shape
    part_local = centroids.shape[0]
    columns = centroids.shape[1]
    capacity = 2 * rows_dev // owners
    owner_of = assign // part_local
    owner_mask = owner_of[:, None] == jnp.arange(owners, dtype=jnp.int32)[None, :]
    counts = jnp.sum(owner_mask.astype(jnp.int32), axis=0)
    starts = jnp.cumsum(counts) - counts
    first_row_index = jnp.sum(jnp.where(owner_mask, starts[None, :], 0), axis=1)
    position = jnp.arange(rows_dev, dtype=jnp.int32) - first_row_index
    slot_index = owner_of * capacity + position
    source_rows = starts[:, None] + jnp.arange(capacity, dtype=jnp.int32)[None, :]
    usable_slot = jnp.arange(capacity, dtype=jnp.int32)[None, :] < counts[:, None]
    clipped = jnp.minimum(source_rows, rows_dev - 1)
    send_rows = jnp.where(
        usable_slot[:, :, None], jnp.take(vectors, clipped, axis=0), jnp.zeros((), jnp.bfloat16)
    )
    owner_base = (jnp.arange(owners, dtype=jnp.int32) * part_local)[:, None]
    send_ids = jnp.where(usable_slot, jnp.take(assign, clipped, axis=0) - owner_base, part_local)
    split_rows = send_rows.reshape(owners, capacity, sub_count, columns).transpose(0, 2, 1, 3)
    split_rows = split_rows.reshape(owners * sub_count, capacity, columns)
    id_copies = jnp.broadcast_to(send_ids[:, None, :], (owners, sub_count, capacity)).reshape(
        owners * sub_count, capacity
    )
    arrived, arrived_ids = (
        lax.all_to_all(split_rows, ("dom", "sub"), split_axis=0, concat_axis=0, tiled=True),
        lax.all_to_all(id_copies, ("dom", "sub"), split_axis=0, concat_axis=0, tiled=True),
    )
    arrived = arrived.reshape(-1, columns)
    slot_ids = arrived_ids.reshape(-1)
    usable = slot_ids < part_local
    safe_ids = jnp.minimum(slot_ids, part_local - 1)
    as_float = arrived.astype(jnp.float32)
    arrived_count = arrived.shape[0]
    block = 512
    block_count = arrived_count // block
    id_blocks = slot_ids.reshape(block_count, block)
    row_blocks = arrived.reshape(block_count, block, columns)
    part_range = jnp.arange(part_local, dtype=jnp.int32)
    contract_rows = (((0,), (0,)), ((), ()))

    def member_table(ids):
        return (ids[:, None] == part_range[None, :]).astype(jnp.bfloat16)

    def tally_step(carry, inputs):
        ids, rows_b = inputs
        table = member_table(ids)
        count_acc, sum_acc = carry
        count_acc = count_acc + jnp.sum(table, axis=0, dtype=jnp.float32)
        sum_acc = sum_acc + lax.dot_general(
            table, rows_b, contract_rows, preferred_element_type=jnp.float32
        )
        return ((count_acc, sum_acc), None)

    start_tally = (
        jnp.zeros((part_local,), jnp.float32),
        jnp.zeros((part_local, columns), jnp.float32),
    )
    (filled, sum_x), unused = lax.scan(tally_step, start_tally, (id_blocks, row_blocks))

    def project_step(acc, inputs):
        ids, rows_b, weight_b = inputs
        table = member_table(ids).astype(jnp.float32)
        scaled = rows_b.astype(jnp.float32) * weight_b[:, None]
        term = lax.dot_general(
            table,
            scaled,
            contract_rows,
            precision=lax.Precision.HIGHEST,
            preferred_element_type=jnp.float32,
        )
        return (acc + term, None)

    norms = lax.psum(jnp.sum(as_float * as_float, axis=1), "sub")
    floors = jnp.maximum(filled, 1.0)[:, None]
    weight_fractions = perp_ratio[:, None]
    current = centroids
    for iteration in range(ITERS):
        picked = jnp.take(current, safe_ids, axis=0)
        inner_full = lax.psum(jnp.sum(as_float * picked, axis=1), "sub")
        weight = inner_full / (norms + 1e-06)
        weight_blocks = weight.reshape(block_count, block)
        projected, unused = lax.scan(
            project_step,
            jnp.zeros((part_local, columns), jnp.float32),
            (id_blocks, row_blocks, weight_blocks),
        )
        current = (
            current
            - (
                weight_fractions * filled[:, None] * current
                + (1.0 - weight_fractions) * projected
                - sum_x
            )
            / floors
        )
    picked = jnp.take(current, safe_ids, axis=0)
    residual = jnp.where(usable[:, None], as_float - picked, 0.0).astype(jnp.bfloat16)
    residual = residual.reshape(owners, sub_count * capacity, columns)
    outgoing = residual.reshape(owners * sub_count, capacity, columns)
    returned = lax.all_to_all(outgoing, ("dom", "sub"), split_axis=0, concat_axis=0, tiled=True)
    returned = returned.reshape(owners, sub_count, capacity, columns).transpose(0, 2, 1, 3)
    flat_rows = returned.reshape(owners * capacity, row_width)
    residual_rows = jnp.take(flat_rows, slot_index, axis=0)
    m_all = codes.shape[1]
    code_range = jnp.arange(K, dtype=jnp.int32)
    code_member = (codes[:, :, None] == code_range[None, None, :]).astype(jnp.bfloat16)
    pieces = residual_rows.reshape(rows_dev, m_all, DS)
    book_sums = jnp.einsum(
        "rmk,rmd->mkd", code_member, pieces, preferred_element_type=jnp.float32
    ).reshape(m_all * K, DS)
    book_counts = jnp.sum(code_member, axis=0, dtype=jnp.float32).reshape(m_all * K)
    local_sub = codebook.shape[0]
    all_sums, all_counts = lax.psum((book_sums, book_counts), ("dom", "sub"))
    offset = lax.axis_index("sub") * (local_sub * K)
    totals = lax.dynamic_slice_in_dim(all_sums, offset, local_sub * K, 0)
    tallies = lax.dynamic_slice_in_dim(all_counts, offset, local_sub * K, 0)
    weights = codeword_weight_total.reshape(local_sub * K, 1)
    updated = (codebook.reshape(local_sub * K, DS) * weights + totals) / (
        weights + tallies[:, None]
    )
    return (current, residual_rows, updated.reshape(local_sub, K, DS))


def solution(mesh):
    placed = (
        P(("dom", "sub"), None),
        P(("dom", "sub")),
        P(("dom", "sub"), None),
        P("dom", "sub"),
        P("dom"),
        P("sub", None, None),
        P("sub", None),
    )
    return jax.shard_map(
        per_device,
        mesh=mesh,
        in_specs=placed,
        out_specs=(P("dom", "sub"), P(("dom", "sub"), None), P("sub", None, None)),
        check_vma=False,
    )
```

profile of v0, /device:TPU:1, one launch (start us, length us, event | category | flops | bytes accessed | tf_op | source)
XLA Modules:
  0.0 561.8 jit_solution(17518473978738521301)
XLA Ops:
  31.1 10.8 %gather_fusion.3 = f32[2048,256]{1,0:T(8,128)} fusion(f32[4096,256]{1,0:T(8,128)} %param.22, s32[2048]{0:T(1024)S(1)} %fusion.58), kind=kCustom, calls=%fused_computation.clone | custom fusion | bytes 4202496 | tf_op jit(solution)/shard_map/jit(_take)/gather | solution.py:92
  41.9 14.1 %all-to-all-done.1 = bf16[32,64,256]{2,1,0:T(8,128)(2,1)S(1)} async-done(((bf16[32,64,256]{2,1,0:T(8,128)(2,1)}), bf16[32,64,256]{2,1,0:T(8,128)(2,1)S(1)}, u32[]{:S(2)}, u32[]{:S(2)}) %all-to-all-start.1) | async-done | bytes 1048608 | tf_op jit(solution)/shard_map/all_to_all | solution.py:39
  58.4 13.2 %all-reduce = (f32[2048]{0:T(1024)S(1)}, f32[2048]{0:T(1024)S(1)}) all-reduce(f32[2048]{0:T(1024)S(1)} %fusion.48, f32[2048]{0:T(1024)S(1)} %reduce_sum.86), channel_id=1, replica_groups=mesh['dom'=8,'sub'=4] {'sub'}, use_global_device_ids=true, to_apply=%region_6.8 | all-reduce | flops 4096 | bytes 32768 | tf_op jit(solution)/shard_map/psum | solution.py:93
  71.7 39.2 %while.58 = (s32[]{:T(128)}, f32[4096,256]{1,0:T(8,128)}, s32[4,512]{1,0:T(4,128)S(1)}, bf16[4,512,256]{2,1,0:T(8,128)(2,1)S(1)}, f32[4,512]{1,0:T(4,128)S(1)}, /*index=5*/s32[]{:T(128)}, s32[]{:T(128)}) while((s32[]{:T(128)}, f32[4096,256]{1,0:T(8,128)}, s32[4,512]{1,0:T(4,128)S(1)}, bf16[4,512,256]{2,1,0:T(8,128)(2,1)S(1)}, ...), condition=%wide.region_10.12_spmd.clone, body=%wide.region_9.11_spmd.clone.sunk | while | flops 6446907392 | bytes 8663139 | solution.py:96
  80.3 10.2 %fusion.73 = f32[4096,256]{1,0:T(8,128)} fusion(f32[4096,256]{1,0:T(8,128)} %get-tuple-element.532, s32[512]{0:T(512)S(1)} %bitcast.114, pred[]{:T(512)S(6)} %compare.18, f32[512]{0:T(512)S(1)} %bitcast.120, bf16[4,512,256]{2,1,0:T(8,128)(2,1)S(1)} %get-tuple-element.541, s32[]{:T(128)} %get-tuple-element.531), kind=kOutput, calls=%fused_computation.26.clone.1 | convolution fusion | flops 6446907392 | bytes 8654853 | tf_op jit(solution)/shard_map/while/body/eval_jaxpr/dot_general | solution.py:78
  90.5 10.2 %fusion.73 = f32[4096,256]{1,0:T(8,128)} fusion(f32[4096,256]{1,0:T(8,128)} %get-tuple-element.532, s32[512]{0:T(512)S(1)} %bitcast.114, pred[]{:T(512)S(6)} %compare.18, f32[512]{0:T(512)S(1)} %bitcast.120, bf16[4,512,256]{2,1,0:T(8,128)(2,1)S(1)} %get-tuple-element.541, s32[]{:T(128)} %get-tuple-element.531), kind=kOutput, calls=%fused_computation.26.clone.1 | convolution fusion | flops 6446907392 | bytes 8654853 | tf_op jit(solution)/shard_map/while/body/eval_jaxpr/dot_general | solution.py:78
  100.7 10.2 %fusion.73 = f32[4096,256]{1,0:T(8,128)} fusion(f32[4096,256]{1,0:T(8,128)} %get-tuple-element.532, s32[512]{0:T(512)S(1)} %bitcast.114, pred[]{:T(512)S(6)} %compare.18, f32[512]{0:T(512)S(1)} %bitcast.120, bf16[4,512,256]{2,1,0:T(8,128)(2,1)S(1)} %get-tuple-element.541, s32[]{:T(128)} %get-tuple-element.531), kind=kOutput, calls=%fused_computation.26.clone.1 | convolution fusion | flops 6446907392 | bytes 8654853 | tf_op jit(solution)/shard_map/while/body/eval_jaxpr/dot_general | solution.py:78
  110.8 32.9 %while.57 = (s32[]{:T(128)}, f32[4096]{0:T(1024)S(1)}, f32[4096,256]{1,0:T(8,128)}, s32[4,512]{1,0:T(4,128)S(1)}, bf16[4,512,256]{2,1,0:T(8,128)(2,1)S(1)}, /*index=5*/s32[]{:T(128)}, s32[]{:T(128)}) while((s32[]{:T(128)}, f32[4096]{0:T(1024)S(1)}, f32[4096,256]{1,0:T(8,128)}, s32[4,512]{1,0:T(4,128)S(1)}, ...), condition=%wide.region_4.5_spmd.clone, body=%wide.region_2.4_spmd.clone.sunk | while | flops 1086328832 | bytes 8724576 | solution.py:72
  152.3 10.7 %gather_fusion.4 = f32[2048,256]{1,0:T(8,128)} fusion(f32[4096,256]{1,0:T(8,128)} %divide_subtract_fusion.3, s32[2048]{0:T(1024)S(1)} %fusion.58), kind=kCustom, calls=%fused_computation.1.clone | custom fusion | bytes 4202496 | tf_op jit(solution)/shard_map/jit(_take)/gather | solution.py:92
  172.0 39.2 %while.59 = (s32[]{:T(128)}, f32[4096,256]{1,0:T(8,128)}, s32[4,512]{1,0:T(4,128)S(1)}, bf16[4,512,256]{2,1,0:T(8,128)(2,1)S(1)}, f32[4,512]{1,0:T(4,128)S(1)}, /*index=5*/s32[]{:T(128)}, s32[]{:T(128)}) while((s32[]{:T(128)}, f32[4096,256]{1,0:T(8,128)}, s32[4,512]{1,0:T(4,128)S(1)}, bf16[4,512,256]{2,1,0:T(8,128)(2,1)S(1)}, ...), condition=%wide.region_14.16_spmd.clone, body=%wide.region_13.15_spmd.clone.sunk | while | flops 6446907392 | bytes 8663139 | solution.py:96
  180.7 10.2 %fusion.74 = f32[4096,256]{1,0:T(8,128)} fusion(f32[4096,256]{1,0:T(8,128)} %get-tuple-element.553, s32[512]{0:T(512)S(1)} %bitcast.117, pred[]{:T(512)S(6)} %compare.19, f32[512]{0:T(512)S(1)} %bitcast.121, bf16[4,512,256]{2,1,0:T(8,128)(2,1)S(1)} %get-tuple-element.562, s32[]{:T(128)} %get-tuple-element.552), kind=kOutput, calls=%fused_computation.37.clone.1 | convolution fusion | flops 6446907392 | bytes 8654853 | tf_op jit(solution)/shard_map/while/body/eval_jaxpr/dot_general | solution.py:78
  190.9 10.2 %fusion.74 = f32[4096,256]{1,0:T(8,128)} fusion(f32[4096,256]{1,0:T(8,128)} %get-tuple-element.553, s32[512]{0:T(512)S(1)} %bitcast.117, pred[]{:T(512)S(6)} %compare.19, f32[512]{0:T(512)S(1)} %bitcast.121, bf16[4,512,256]{2,1,0:T(8,128)(2,1)S(1)} %get-tuple-element.562, s32[]{:T(128)} %get-tuple-element.552), kind=kOutput, calls=%fused_computation.37.clone.1 | convolution fusion | flops 6446907392 | bytes 8654853 | tf_op jit(solution)/shard_map/while/body/eval_jaxpr/dot_general | solution.py:78
  201.0 10.2 %fusion.74 = f32[4096,256]{1,0:T(8,128)} fusion(f32[4096,256]{1,0:T(8,128)} %get-tuple-element.553, s32[512]{0:T(512)S(1)} %bitcast.117, pred[]{:T(512)S(6)} %compare.19, f32[512]{0:T(512)S(1)} %bitcast.121, bf16[4,512,256]{2,1,0:T(8,128)(2,1)S(1)} %get-tuple-element.562, s32[]{:T(128)} %get-tuple-element.552), kind=kOutput, calls=%fused_computation.37.clone.1 | convolution fusion | flops 6446907392 | bytes 8654853 | tf_op jit(solution)/shard_map/while/body/eval_jaxpr/dot_general | solution.py:78
  219.8 10.7 %gather_fusion.5 = f32[2048,256]{1,0:T(8,128)} fusion(f32[4096,256]{1,0:T(8,128)} %divide_subtract_fusion.2, s32[2048]{0:T(1024)S(1)} %fusion.58), kind=kCustom, calls=%fused_computation.2.clone | custom fusion | bytes 4202496 | tf_op jit(solution)/shard_map/jit(_take)/gather | solution.py:92
  240.8 39.4 %while.60 = (s32[]{:T(128)}, f32[4096,256]{1,0:T(8,128)}, s32[4,512]{1,0:T(4,128)S(1)}, bf16[4,512,256]{2,1,0:T(8,128)(2,1)S(1)}, f32[4,512]{1,0:T(4,128)S(1)}, /*index=5*/s32[]{:T(128)}, s32[]{:T(128)}) while((s32[]{:T(128)}, f32[4096,256]{1,0:T(8,128)}, s32[4,512]{1,0:T(4,128)S(1)}, bf16[4,512,256]{2,1,0:T(8,128)(2,1)S(1)}, ...), condition=%wide.region_18.20_spmd.clone, body=%wide.region_17.19_spmd.clone.sunk | while | flops 6446907392 | bytes 8663139 | solution.py:96
  249.5 10.2 %fusion.75 = f32[4096,256]{1,0:T(8,128)} fusion(f32[4096,256]{1,0:T(8,128)} %get-tuple-element.574, s32[512]{0:T(512)S(1)} %bitcast.118, pred[]{:T(512)S(6)} %compare.20, f32[512]{0:T(512)S(1)} %bitcast.122, bf16[4,512,256]{2,1,0:T(8,128)(2,1)S(1)} %get-tuple-element.583, s32[]{:T(128)} %get-tuple-element.573), kind=kOutput, calls=%fused_computation.48.clone.1 | convolution fusion | flops 6446907392 | bytes 8654853 | tf_op jit(solution)/shard_map/while/body/eval_jaxpr/dot_general | solution.py:78
  259.7 10.2 %fusion.75 = f32[4096,256]{1,0:T(8,128)} fusion(f32[4096,256]{1,0:T(8,128)} %get-tuple-element.574, s32[512]{0:T(512)S(1)} %bitcast.118, pred[]{:T(512)S(6)} %compare.20, f32[512]{0:T(512)S(1)} %bitcast.122, bf16[4,512,256]{2,1,0:T(8,128)(2,1)S(1)} %get-tuple-element.583, s32[]{:T(128)} %get-tuple-element.573), kind=kOutput, calls=%fused_computation.48.clone.1 | convolution fusion | flops 6446907392 | bytes 8654853 | tf_op jit(solution)/shard_map/while/body/eval_jaxpr/dot_general | solution.py:78
  269.9 10.2 %fusion.75 = f32[4096,256]{1,0:T(8,128)} fusion(f32[4096,256]{1,0:T(8,128)} %get-tuple-element.574, s32[512]{0:T(512)S(1)} %bitcast.118, pred[]{:T(512)S(6)} %compare.20, f32[512]{0:T(512)S(1)} %bitcast.122, bf16[4,512,256]{2,1,0:T(8,128)(2,1)S(1)} %get-tuple-element.583, s32[]{:T(128)} %get-tuple-element.573), kind=kOutput, calls=%fused_computation.48.clone.1 | convolution fusion | flops 6446907392 | bytes 8654853 | tf_op jit(solution)/shard_map/while/body/eval_jaxpr/dot_general | solution.py:78
  288.7 10.8 %gather_fusion.6 = f32[2048,256]{1,0:T(8,128)} fusion(f32[4096,256]{1,0:T(8,128)} %divide_subtract_fusion.1, s32[2048]{0:T(1024)S(1)} %fusion.58), kind=kCustom, calls=%fused_computation.3.clone | custom fusion | bytes 4202496 | tf_op jit(solution)/shard_map/jit(_take)/gather | solution.py:92
  308.5 39.2 %while.61 = (s32[]{:T(128)}, f32[4096,256]{1,0:T(8,128)}, s32[4,512]{1,0:T(4,128)S(1)}, bf16[4,512,256]{2,1,0:T(8,128)(2,1)S(1)}, f32[4,512]{1,0:T(4,128)S(1)}, /*index=5*/s32[]{:T(128)}, s32[]{:T(128)}) while((s32[]{:T(128)}, f32[4096,256]{1,0:T(8,128)}, s32[4,512]{1,0:T(4,128)S(1)}, bf16[4,512,256]{2,1,0:T(8,128)(2,1)S(1)}, ...), condition=%wide.region_22.24_spmd.clone, body=%wide.region_21.23_spmd.clone.sunk | while | flops 6446907392 | bytes 8663139 | solution.py:96
  356.1 10.7 %gather_fusion.7 = f32[2048,256]{1,0:T(8,128)} fusion(f32[4096,256]{1,0:T(8,128)} %divide_subtract_fusion, s32[2048]{0:T(1024)S(1)} %fusion.58), kind=kCustom, calls=%fused_computation.4.clone | custom fusion | bytes 4202496 | tf_op jit(solution)/shard_map/jit(_take)/gather | solution.py:110
  369.7 13.6 %all-to-all-start.2 = ((bf16[32,64,256]{2,1,0:T(8,128)(2,1)}), bf16[32,64,256]{2,1,0:T(8,128)(2,1)S(1)}, u32[]{:S(2)}, u32[]{:S(2)}) async-start(bf16[32,64,256]{2,1,0:T(8,128)(2,1)} %bitcast.7), calls=%async_computation.2 | async-start | bytes 2097152 | tf_op jit(solution)/shard_map/all_to_all | solution.py:114
  384.6 43.9 %psum.55 = f32[4096]{0:T(1024)S(1)} all-reduce(f32[4096]{0:T(1024)S(1)} %reshape.297), channel_id=1, replica_groups=mesh['dom'=8,'sub'=4] {'dom','sub'}, use_global_device_ids=true, to_apply=%region_26.28 | all-reduce | flops 4096 | bytes 32768 | tf_op jit(solution)/shard_map/psum | solution.py:127
  434.0 119.1 %all-reduce.3.cloned.1.call-done = f32[4096,4]{0,1:T(4,128)} async-done(((f32[4096,4]{0,1:T(4,128)}), f32[4096,4]{0,1:T(4,128)}) %all-reduce.3.cloned.1.call-update) | async-done | bytes 65552 | tf_op jit(solution)/shard_map/psum | solution.py:127
  (152 shorter events, 197.5 us)
Async XLA Ops:
  7.2 12.9 %copy-start = (bf16[256,1024]{1,0:T(8,128)(2,1)S(1)}, bf16[256,1024]{1,0:T(8,128)(2,1)}, u32[]{:S(2)}) copy-start(bf16[256,1024]{1,0:T(8,128)(2,1)} %param.19) | copy-start | bytes 1572868
  12.8 13.7 %all-to-all-start = ((s32[32,1,64]{2,1,0:T(1,128)}), s32[32,1,64]{2,1,0:T(1,128)S(1)}, u32[]{:S(2)}, u32[]{:S(2)}) async-start(s32[32,1,64]{2,1,0:T(1,128)} %bitcast.2), calls=%async_computation | async-start | bytes 32768 | tf_op jit(solution)/shard_map/all_to_all | solution.py:40
  26.5 29.5 %all-to-all-start.1 = ((bf16[32,64,256]{2,1,0:T(8,128)(2,1)}), bf16[32,64,256]{2,1,0:T(8,128)(2,1)S(1)}, u32[]{:S(2)}, u32[]{:S(2)}) async-start(bf16[32,64,256]{2,1,0:T(8,128)(2,1)} %bitcast.4), calls=%async_computation.1 | async-start | bytes 2097152 | tf_op jit(solution)/shard_map/all_to_all | solution.py:39
  110.8 32.9 %copy-start.5 = (f32[4096]{0:T(1024)S(1)}, f32[4096]{0:T(1024)}, u32[]{:S(2)}) copy-start(f32[4096]{0:T(1024)} %param.23) | copy-start | bytes 49156
  366.9 16.5 %copy-start.3 = (s32[256,256]{1,0:T(8,128)S(1)}, s32[256,256]{1,0:T(8,128)}, u32[]{:S(2)}) copy-start(s32[256,256]{1,0:T(8,128)} %param.21) | copy-start | bytes 786436
  366.9 17.3 %copy-start.6 = (f32[64,16]{0,1:T(8,128)S(1)}, f32[64,16]{0,1:T(8,128)}, u32[]{:S(2)}) copy-start(f32[64,16]{0,1:T(8,128)} %param.25) | copy-start | bytes 12292
  366.9 17.5 %copy-start.4 = (f32[64,16,4]{0,2,1:T(4,128)S(1)}, f32[64,16,4]{0,2,1:T(4,128)}, u32[]{:S(2)}) copy-start(f32[64,16,4]{0,2,1:T(4,128)} %param.24) | copy-start | bytes 49156
  366.9 61.8 %copy-start.2 = (s32[256]{0:T(256)S(1)}, s32[256]{0:T(256)}, u32[]{:S(2)}) copy-start(s32[256]{0:T(256)} %param.20) | copy-start | bytes 3076
  369.7 59.0 %all-to-all-start.2 = ((bf16[32,64,256]{2,1,0:T(8,128)(2,1)}), bf16[32,64,256]{2,1,0:T(8,128)(2,1)S(1)}, u32[]{:S(2)}, u32[]{:S(2)}) async-start(bf16[32,64,256]{2,1,0:T(8,128)(2,1)} %bitcast.7), calls=%async_computation.2 | async-start | bytes 2097152 | tf_op jit(solution)/shard_map/all_to_all | solution.py:114
  383.3 169.9 %all-reduce.3.cloned.1.call-start = ((), (), s32[]{:S(2)}) async-start(), calls=%async_computation.3 | async-start | bytes 131072 | tf_op jit(solution)/shard_map/psum | solution.py:127
  430.9 123.8 %copy-start.1 = (bf16[256,1024]{1,0:T(8,128)(2,1)S(1)}, bf16[256,1024]{1,0:T(8,128)(2,1)}, u32[]{:S(2)}) copy-start(bf16[256,1024]{1,0:T(8,128)(2,1)} %param.19) | copy-start | bytes 1572868
Sparse Core Ops, SparseCore 0:
  433.2 119.8 all-reduce.2
where the time goes:
time: 566 us; the launch traced here: 562 us
  matrix products  182 us (32%)
  waiting for transfers between devices  136 us (24%)
  blocking collectives  79.3 us (14%)
  local copies, waits for them, and re-layouts  66.3 us (12%)
  other arithmetic  59.1 us (10%)
  starting transfers between devices  23.7 us (4%)
  between operations  14.7 us (3%)
    dot_general x16, matrix products, project_step(): lax.dot_general(table, scaled, contract_rows, precision=lax.Precision.HIG...  156 us
    psum x1, waiting for transfers between devices, per_device(): all_sums, all_counts = lax.psum((book_sums, book_counts), ('dom', 'sub'))  119 us
    gather x5, local copies, waits for them, and re-layouts, per_device(): picked = jnp.take(current, safe_ids, axis=0)  53.8 us
    psum x1, blocking collectives, per_device(): all_sums, all_counts = lax.psum((book_sums, book_counts), ('dom', 'sub'))  43.9 us
    psum x4, blocking collectives, per_device(): inner_full = lax.psum(jnp.sum(as_float * picked, axis=1), 'sub')  35.4 us
    sub x4, other arithmetic, per_device(): current - (weight_fractions * filled[:, None] * current + (1.0 - weight_f...  34.2 us
    dot_general x4, matrix products, tally_step(): lax.dot_general(table, rows_b, contract_rows, preferred_element_type=jnp....  24.7 us
    all_to_all x1, waiting for transfers between devices, per_device(): lax.all_to_all(split_rows, ('dom', 'sub'), split_axis=0, concat_axis=0, t...  14.1 us
  transfers between devices with their start and end apart: 4, of which 3 were waited for; matrix products, arithmetic and copies ran while one was open for 3% of the time, Pallas kernels for 0%

commit v1 on v0

--- a/solution.py
+++ b/solution.py
@@ -6,6 +6,11 @@
 K = 16
 DS = 4
 ITERS = 4
+
+
+def one_after_other(array, one, other):
+    inner = lax.psum(array, one)
+    return lax.psum(inner, other)
 
 
 def per_device(vectors, assign, codes, centroids, perp_ratio, codebook, codeword_weight_total):
@@ -124,7 +129,7 @@
     ).reshape(m_all * K, DS)
     book_counts = jnp.sum(code_member, axis=0, dtype=jnp.float32).reshape(m_all * K)
     local_sub = codebook.shape[0]
-    all_sums, all_counts = lax.psum((book_sums, book_counts), ("dom", "sub"))
+    all_sums, all_counts = one_after_other((book_sums, book_counts), "sub", "dom")
     offset = lax.axis_index("sub") * (local_sub * K)
     totals = lax.dynamic_slice_in_dim(all_sums, offset, local_sub * K, 0)
     tallies = lax.dynamic_slice_in_dim(all_counts, offset, local_sub * K, 0)

time: 566 us -> 526 us (0.929)
  waiting for transfers between devices: 136 us -> 109 us
  blocking collectives: 79.3 us -> 63.7 us
    psum x1 -> x2, waiting for transfers between devices: 119 us -> 89.3 us  [the longest x1 55.8 us: one_after_other(): return lax.psum(inner, other)]
    psum x1, blocking collectives: 43.9 us -> 22.8 us  [one_after_other(): return lax.psum(inner, other)]
  transfers between devices with their start and end apart: 4 -> 5, of which waited for: 3 -> 5; matrix products, arithmetic and copies ran while one was open for 3% -> 3% of each run, Pallas kernels for 0% -> 0%
where the time goes in v1:
time: 526 us; the launch traced here: 520 us
  matrix products  182 us (35%)
  waiting for transfers between devices  109 us (21%)
  local copies, waits for them, and re-layouts  66.3 us (13%)
  blocking collectives  63.7 us (12%)
  other arithmetic  59.1 us (11%)
  starting transfers between devices  25.5 us (5%)
  between operations  14.6 us (3%)
    dot_general x16, matrix products, project_step(): lax.dot_general(table, scaled, contract_rows, precision=lax.Precision.HIG...  156 us
    psum x1, waiting for transfers between devices, one_after_other(): return lax.psum(inner, other)  55.8 us
    gather x5, local copies, waits for them, and re-layouts, per_device(): picked = jnp.take(current, safe_ids, axis=0)  53.8 us
    psum x4, blocking collectives, per_device(): inner_full = lax.psum(jnp.sum(as_float * picked, axis=1), 'sub')  40.9 us
    sub x4, other arithmetic, per_device(): current - (weight_fractions * filled[:, None] * current + (1.0 - weight_f...  34.2 us
    psum x1, waiting for transfers between devices, one_after_other(): inner = lax.psum(array, one)  33.5 us
    dot_general x4, matrix products, tally_step(): lax.dot_general(table, rows_b, contract_rows, preferred_element_type=jnp....  24.7 us
    psum x1, blocking collectives, one_after_other(): return lax.psum(inner, other)  22.8 us
  transfers between devices with their start and end apart: 5, of which 5 were waited for; matrix products, arithmetic and copies ran while one was open for 3% of the time, Pallas kernels for 0%

profile of v1, /device:TPU:1, one launch (start us, length us, event | category | flops | bytes accessed | tf_op | source)
XLA Modules:
  0.0 520.1 jit_solution(15418528127494719410)
XLA Ops:
  32.0 10.8 %gather_fusion.3 = f32[2048,256]{1,0:T(8,128)} fusion(f32[4096,256]{1,0:T(8,128)} %param.22, s32[2048]{0:T(1024)S(1)} %fusion.58), kind=kCustom, calls=%fused_computation.clone | custom fusion | bytes 4202496 | tf_op jit(solution)/shard_map/jit(_take)/gather | solution.py:97
  42.8 13.2 %all-to-all-done.1 = bf16[32,64,256]{2,1,0:T(8,128)(2,1)S(1)} async-done(((bf16[32,64,256]{2,1,0:T(8,128)(2,1)}), bf16[32,64,256]{2,1,0:T(8,128)(2,1)S(1)}, u32[]{:S(2)}, u32[]{:S(2)}) %all-to-all-start.1) | async-done | bytes 1048608 | tf_op jit(solution)/shard_map/all_to_all | solution.py:44
  58.4 13.2 %all-reduce.1 = (f32[2048]{0:T(1024)S(1)}, f32[2048]{0:T(1024)S(1)}) all-reduce(f32[2048]{0:T(1024)S(1)} %fusion.48, f32[2048]{0:T(1024)S(1)} %reduce_sum.86), channel_id=1, replica_groups=mesh['dom'=8,'sub'=4] {'sub'}, use_global_device_ids=true, to_apply=%region_6.8 | all-reduce | flops 4096 | bytes 32768 | tf_op jit(solution)/shard_map/psum | solution.py:98
  71.7 39.2 %while.58 = (s32[]{:T(128)}, f32[4096,256]{1,0:T(8,128)}, s32[4,512]{1,0:T(4,128)S(1)}, bf16[4,512,256]{2,1,0:T(8,128)(2,1)S(1)}, f32[4,512]{1,0:T(4,128)S(1)}, /*index=5*/s32[]{:T(128)}, s32[]{:T(128)}) while((s32[]{:T(128)}, f32[4096,256]{1,0:T(8,128)}, s32[4,512]{1,0:T(4,128)S(1)}, bf16[4,512,256]{2,1,0:T(8,128)(2,1)S(1)}, ...), condition=%wide.region_10.12_spmd.clone, body=%wide.region_9.11_spmd.clone.sunk | while | flops 6446907392 | bytes 8663139 | solution.py:101
  80.3 10.2 %fusion.73 = f32[4096,256]{1,0:T(8,128)} fusion(f32[4096,256]{1,0:T(8,128)} %get-tuple-element.534, s32[512]{0:T(512)S(1)} %bitcast.114, pred[]{:T(512)S(6)} %compare.18, f32[512]{0:T(512)S(1)} %bitcast.120, bf16[4,512,256]{2,1,0:T(8,128)(2,1)S(1)} %get-tuple-element.543, s32[]{:T(128)} %get-tuple-element.533), kind=kOutput, calls=%fused_computation.26.clone.1 | convolution fusion | flops 6446907392 | bytes 8654853 | tf_op jit(solution)/shard_map/while/body/eval_jaxpr/dot_general | solution.py:83
  90.5 10.2 %fusion.73 = f32[4096,256]{1,0:T(8,128)} fusion(f32[4096,256]{1,0:T(8,128)} %get-tuple-element.534, s32[512]{0:T(512)S(1)} %bitcast.114, pred[]{:T(512)S(6)} %compare.18, f32[512]{0:T(512)S(1)} %bitcast.120, bf16[4,512,256]{2,1,0:T(8,128)(2,1)S(1)} %get-tuple-element.543, s32[]{:T(128)} %get-tuple-element.533), kind=kOutput, calls=%fused_computation.26.clone.1 | convolution fusion | flops 6446907392 | bytes 8654853 | tf_op jit(solution)/shard_map/while/body/eval_jaxpr/dot_general | solution.py:83
  110.8 32.9 %while.57 = (s32[]{:T(128)}, f32[4096]{0:T(1024)S(1)}, f32[4096,256]{1,0:T(8,128)}, s32[4,512]{1,0:T(4,128)S(1)}, bf16[4,512,256]{2,1,0:T(8,128)(2,1)S(1)}, /*index=5*/s32[]{:T(128)}, s32[]{:T(128)}) while((s32[]{:T(128)}, f32[4096]{0:T(1024)S(1)}, f32[4096,256]{1,0:T(8,128)}, s32[4,512]{1,0:T(4,128)S(1)}, ...), condition=%wide.region_4.5_spmd.clone, body=%wide.region_2.4_spmd.clone.sunk | while | flops 1086328832 | bytes 8724576 | solution.py:77
  152.3 10.7 %gather_fusion.4 = f32[2048,256]{1,0:T(8,128)} fusion(f32[4096,256]{1,0:T(8,128)} %divide_subtract_fusion.3, s32[2048]{0:T(1024)S(1)} %fusion.58), kind=kCustom, calls=%fused_computation.1.clone | custom fusion | bytes 4202496 | tf_op jit(solution)/shard_map/jit(_take)/gather | solution.py:97
  172.0 39.2 %while.59 = (s32[]{:T(128)}, f32[4096,256]{1,0:T(8,128)}, s32[4,512]{1,0:T(4,128)S(1)}, bf16[4,512,256]{2,1,0:T(8,128)(2,1)S(1)}, f32[4,512]{1,0:T(4,128)S(1)}, /*index=5*/s32[]{:T(128)}, s32[]{:T(128)}) while((s32[]{:T(128)}, f32[4096,256]{1,0:T(8,128)}, s32[4,512]{1,0:T(4,128)S(1)}, bf16[4,512,256]{2,1,0:T(8,128)(2,1)S(1)}, ...), condition=%wide.region_14.16_spmd.clone, body=%wide.region_13.15_spmd.clone.sunk | while | flops 6446907392 | bytes 8663139 | solution.py:101
  180.7 10.2 %fusion.74 = f32[4096,256]{1,0:T(8,128)} fusion(f32[4096,256]{1,0:T(8,128)} %get-tuple-element.555, s32[512]{0:T(512)S(1)} %bitcast.117, pred[]{:T(512)S(6)} %compare.19, f32[512]{0:T(512)S(1)} %bitcast.121, bf16[4,512,256]{2,1,0:T(8,128)(2,1)S(1)} %get-tuple-element.564, s32[]{:T(128)} %get-tuple-element.554), kind=kOutput, calls=%fused_computation.37.clone.1 | convolution fusion | flops 6446907392 | bytes 8654853 | tf_op jit(solution)/shard_map/while/body/eval_jaxpr/dot_general | solution.py:83
  201.0 10.2 %fusion.74 = f32[4096,256]{1,0:T(8,128)} fusion(f32[4096,256]{1,0:T(8,128)} %get-tuple-element.555, s32[512]{0:T(512)S(1)} %bitcast.117, pred[]{:T(512)S(6)} %compare.19, f32[512]{0:T(512)S(1)} %bitcast.121, bf16[4,512,256]{2,1,0:T(8,128)(2,1)S(1)} %get-tuple-element.564, s32[]{:T(128)} %get-tuple-element.554), kind=kOutput, calls=%fused_computation.37.clone.1 | convolution fusion | flops 6446907392 | bytes 8654853 | tf_op jit(solution)/shard_map/while/body/eval_jaxpr/dot_general | solution.py:83
  219.8 10.7 %gather_fusion.5 = f32[2048,256]{1,0:T(8,128)} fusion(f32[4096,256]{1,0:T(8,128)} %divide_subtract_fusion.2, s32[2048]{0:T(1024)S(1)} %fusion.58), kind=kCustom, calls=%fused_computation.2.clone | custom fusion | bytes 4202496 | tf_op jit(solution)/shard_map/jit(_take)/gather | solution.py:97
  240.8 39.4 %while.60 = (s32[]{:T(128)}, f32[4096,256]{1,0:T(8,128)}, s32[4,512]{1,0:T(4,128)S(1)}, bf16[4,512,256]{2,1,0:T(8,128)(2,1)S(1)}, f32[4,512]{1,0:T(4,128)S(1)}, /*index=5*/s32[]{:T(128)}, s32[]{:T(128)}) while((s32[]{:T(128)}, f32[4096,256]{1,0:T(8,128)}, s32[4,512]{1,0:T(4,128)S(1)}, bf16[4,512,256]{2,1,0:T(8,128)(2,1)S(1)}, ...), condition=%wide.region_18.20_spmd.clone, body=%wide.region_17.19_spmd.clone.sunk | while | flops 6446907392 | bytes 8663139 | solution.py:101
  249.5 10.2 %fusion.75 = f32[4096,256]{1,0:T(8,128)} fusion(f32[4096,256]{1,0:T(8,128)} %get-tuple-element.576, s32[512]{0:T(512)S(1)} %bitcast.118, pred[]{:T(512)S(6)} %compare.20, f32[512]{0:T(512)S(1)} %bitcast.122, bf16[4,512,256]{2,1,0:T(8,128)(2,1)S(1)} %get-tuple-element.585, s32[]{:T(128)} %get-tuple-element.575), kind=kOutput, calls=%fused_computation.48.clone.1 | convolution fusion | flops 6446907392 | bytes 8654853 | tf_op jit(solution)/shard_map/while/body/eval_jaxpr/dot_general | solution.py:83
  259.7 10.2 %fusion.75 = f32[4096,256]{1,0:T(8,128)} fusion(f32[4096,256]{1,0:T(8,128)} %get-tuple-element.576, s32[512]{0:T(512)S(1)} %bitcast.118, pred[]{:T(512)S(6)} %compare.20, f32[512]{0:T(512)S(1)} %bitcast.122, bf16[4,512,256]{2,1,0:T(8,128)(2,1)S(1)} %get-tuple-element.585, s32[]{:T(128)} %get-tuple-element.575), kind=kOutput, calls=%fused_computation.48.clone.1 | convolution fusion | flops 6446907392 | bytes 8654853 | tf_op jit(solution)/shard_map/while/body/eval_jaxpr/dot_general | solution.py:83
  269.9 10.2 %fusion.75 = f32[4096,256]{1,0:T(8,128)} fusion(f32[4096,256]{1,0:T(8,128)} %get-tuple-element.576, s32[512]{0:T(512)S(1)} %bitcast.118, pred[]{:T(512)S(6)} %compare.20, f32[512]{0:T(512)S(1)} %bitcast.122, bf16[4,512,256]{2,1,0:T(8,128)(2,1)S(1)} %get-tuple-element.585, s32[]{:T(128)} %get-tuple-element.575), kind=kOutput, calls=%fused_computation.48.clone.1 | convolution fusion | flops 6446907392 | bytes 8654853 | tf_op jit(solution)/shard_map/while/body/eval_jaxpr/dot_general | solution.py:83
  288.7 10.8 %gather_fusion.6 = f32[2048,256]{1,0:T(8,128)} fusion(f32[4096,256]{1,0:T(8,128)} %divide_subtract_fusion.1, s32[2048]{0:T(1024)S(1)} %fusion.58), kind=kCustom, calls=%fused_computation.3.clone | custom fusion | bytes 4202496 | tf_op jit(solution)/shard_map/jit(_take)/gather | solution.py:97
  301.4 12.5 %all-reduce = (f32[2048]{0:T(1024)S(1)}, f32[4096]{0:T(1024)S(1)}) all-reduce(f32[2048]{0:T(1024)S(1)} %fusion.51, f32[4096]{0:T(1024)S(1)} %reshape.297), channel_id=1, replica_groups=mesh['dom'=8,'sub'=4] {'sub'}, use_global_device_ids=true, to_apply=%region_20.22 | all-reduce | flops 6144 | bytes 49152 | tf_op jit(solution)/shard_map/psum | solution.py:98
  314.0 39.2 %while.61 = (s32[]{:T(128)}, f32[4096,256]{1,0:T(8,128)}, s32[4,512]{1,0:T(4,128)S(1)}, bf16[4,512,256]{2,1,0:T(8,128)(2,1)S(1)}, f32[4,512]{1,0:T(4,128)S(1)}, /*index=5*/s32[]{:T(128)}, s32[]{:T(128)}) while((s32[]{:T(128)}, f32[4096,256]{1,0:T(8,128)}, s32[4,512]{1,0:T(4,128)S(1)}, bf16[4,512,256]{2,1,0:T(8,128)(2,1)S(1)}, ...), condition=%wide.region_22.24_spmd.clone, body=%wide.region_21.23_spmd.clone.sunk | while | flops 6446907392 | bytes 8663139 | solution.py:101
  361.6 10.7 %gather_fusion.7 = f32[2048,256]{1,0:T(8,128)} fusion(f32[4096,256]{1,0:T(8,128)} %divide_subtract_fusion, s32[2048]{0:T(1024)S(1)} %fusion.58), kind=kCustom, calls=%fused_computation.4.clone | custom fusion | bytes 4202496 | tf_op jit(solution)/shard_map/jit(_take)/gather | solution.py:115
  375.2 15.3 %all-to-all-start.2 = ((bf16[32,64,256]{2,1,0:T(8,128)(2,1)}), bf16[32,64,256]{2,1,0:T(8,128)(2,1)S(1)}, u32[]{:S(2)}, u32[]{:S(2)}) async-start(bf16[32,64,256]{2,1,0:T(8,128)(2,1)} %bitcast.7), calls=%async_computation.2 | async-start | bytes 2097152 | tf_op jit(solution)/shard_map/all_to_all | solution.py:119
  391.0 22.8 %psum.71 = f32[4096]{0:T(1024)S(1)} all-reduce(f32[4096]{0:T(1024)S(1)} %get-tuple-element.336), channel_id=1, replica_groups=mesh['dom'=8,'sub'=4] {'dom'}, use_global_device_ids=true, to_apply=%region_28.30 | all-reduce | flops 4096 | bytes 32768 | tf_op jit(solution)/shard_map/psum | solution.py:13
  421.3 33.5 %all-reduce.5.cloned.1.call-done = f32[4096,4]{0,1:T(4,128)} async-done(((f32[4096,4]{0,1:T(4,128)}), f32[4096,4]{0,1:T(4,128)}) %all-reduce.5.cloned.1.call-update) | async-done | bytes 65552 | tf_op jit(solution)/shard_map/psum | solution.py:12
  455.7 55.8 %all-reduce.7.cloned.1.call-done = f32[4096,4]{0,1:T(4,128)} async-done(((f32[4096,4]{0,1:T(4,128)}), f32[4096,4]{0,1:T(4,128)}) %all-reduce.7.cloned.1.call-update) | async-done | bytes 65552 | tf_op jit(solution)/shard_map/psum | solution.py:13
  (155 shorter events, 213.8 us)
Async XLA Ops:
  7.2 12.9 %copy-start = (bf16[256,1024]{1,0:T(8,128)(2,1)S(1)}, bf16[256,1024]{1,0:T(8,128)(2,1)}, u32[]{:S(2)}) copy-start(bf16[256,1024]{1,0:T(8,128)(2,1)} %param.19) | copy-start | bytes 1572868
  12.8 13.7 %all-to-all-start = ((s32[32,1,64]{2,1,0:T(1,128)}), s32[32,1,64]{2,1,0:T(1,128)S(1)}, u32[]{:S(2)}, u32[]{:S(2)}) async-start(s32[32,1,64]{2,1,0:T(1,128)} %bitcast.2), calls=%async_computation | async-start | bytes 32768 | tf_op jit(solution)/shard_map/all_to_all | solution.py:45
  22.1 7.5 %copy-start.3 = (s32[256,256]{1,0:T(8,128)S(1)}, s32[256,256]{1,0:T(8,128)}, u32[]{:S(2)}) copy-start(s32[256,256]{1,0:T(8,128)} %param.21) | copy-start | bytes 786436
  26.5 29.5 %all-to-all-start.1 = ((bf16[32,64,256]{2,1,0:T(8,128)(2,1)}), bf16[32,64,256]{2,1,0:T(8,128)(2,1)S(1)}, u32[]{:S(2)}, u32[]{:S(2)}) async-start(bf16[32,64,256]{2,1,0:T(8,128)(2,1)} %bitcast.4), calls=%async_computation.1 | async-start | bytes 2097152 | tf_op jit(solution)/shard_map/all_to_all | solution.py:44
  110.8 32.9 %copy-start.5 = (f32[4096]{0:T(1024)S(1)}, f32[4096]{0:T(1024)}, u32[]{:S(2)}) copy-start(f32[4096]{0:T(1024)} %param.23) | copy-start | bytes 49156
  372.4 18.1 %copy-start.6 = (f32[64,16]{0,1:T(8,128)S(1)}, f32[64,16]{0,1:T(8,128)}, u32[]{:S(2)}) copy-start(f32[64,16]{0,1:T(8,128)} %param.25) | copy-start | bytes 12292
  372.4 18.3 %copy-start.4 = (f32[64,16,4]{0,2,1:T(4,128)S(1)}, f32[64,16,4]{0,2,1:T(4,128)}, u32[]{:S(2)}) copy-start(f32[64,16,4]{0,2,1:T(4,128)} %param.24) | copy-start | bytes 49156
  372.4 18.6 %copy-start.2 = (s32[256]{0:T(256)S(1)}, s32[256]{0:T(256)}, u32[]{:S(2)}) copy-start(s32[256]{0:T(256)} %param.20) | copy-start | bytes 3076
  375.2 41.6 %all-to-all-start.2 = ((bf16[32,64,256]{2,1,0:T(8,128)(2,1)}), bf16[32,64,256]{2,1,0:T(8,128)(2,1)S(1)}, u32[]{:S(2)}, u32[]{:S(2)}) async-start(bf16[32,64,256]{2,1,0:T(8,128)(2,1)} %bitcast.7), calls=%async_computation.2 | async-start | bytes 2097152 | tf_op jit(solution)/shard_map/all_to_all | solution.py:119
  390.5 64.3 %all-reduce.5.cloned.1.call-start = ((), (), s32[]{:S(2)}) async-start(), calls=%async_computation.3 | async-start | bytes 131072 | tf_op jit(solution)/shard_map/psum | solution.py:12
  419.0 94.1 %copy-start.1 = (bf16[256,1024]{1,0:T(8,128)(2,1)S(1)}, bf16[256,1024]{1,0:T(8,128)(2,1)}, u32[]{:S(2)}) copy-start(bf16[256,1024]{1,0:T(8,128)(2,1)} %param.19) | copy-start | bytes 1572868
  421.2 90.3 %all-reduce.7.cloned.1.call-start = ((), (), s32[]{:S(2)}) async-start(), calls=%async_computation.4 | async-start | bytes 131072 | tf_op jit(solution)/shard_map/psum | solution.py:13
Sparse Core Ops, SparseCore 0:
  421.4 33.3 all-reduce.4
  458.1 53.3 all-reduce.6
